TPU v7x, 256 devices: a whole 4x4x8 slice. The times are simulated.
256 devices in a mesh: ctx: 16 (over z, core), ch: 16 (over y, x).
Axes of the slice: x: 4, y: 4, z: 8, core: 2. Of those that a mesh axis runs over, the one named last changes fastest.
Arguments:
- inputs: bfloat16 [4096, 4096], P('ctx', 'ch'), may hold values from -6 to 6
- gating: bfloat16 [4096, 4096], P('ctx', 'ch'), may hold values from -6 to 6
- filter_taps: bfloat16 [4096, 4096], P('ctx', 'ch'), may hold values from -2.25 to 2.25
- skip_gain: float32 [4096], P('ch'), may hold values from 0.5 to 1.5
- w_out: bfloat16 [4096, 4096], P('ch'), may hold values from -0.09375 to 0.09375
- cotangent: bfloat16 [4096, 4096], P('ctx', 'ch'), may hold values from -0.3125 to 0.3125
Outputs:
- output: bfloat16 [4096, 4096], P('ctx', 'ch')
- filter_grad: float32 [4096, 4096], P('ctx', 'ch')
All inputs are finite; a program needn't handle non-finite values.
Results may differ from a plain program's by a relative error of at most 0.015.
Values may be sent and summed in bfloat16 or wider, within the bound.
No kernel may reach another device: no remote copies, remote signals or barrier semaphores. Data moves between devices by JAX's collectives and lax.ppermute only.
A program may use at most 64 MiB of HBM per device.

v0:
```python
import math
import jax
import jax.numpy as jnp
from jax import lax
from jax.sharding import PartitionSpec as P

exact_prec = lax.Precision.HIGHEST


def spectral_tables(block_len):
    time_ids = jnp.arange(2 * block_len, dtype=jnp.int32)
    freq_ids = jnp.arange(block_len, dtype=jnp.int32)
    phase_ids = freq_ids[:, None] * time_ids[None, :] % (2 * block_len)
    angles = phase_ids.astype(jnp.float32) * (math.pi / block_len)
    parity = jnp.where(time_ids % 2 == 0, 1.0, -1.0).astype(jnp.float32)[None, :]
    is_first = (freq_ids == 0)[:, None]
    forward = jnp.concatenate(
        [jnp.cos(angles), jnp.where(is_first, parity, -jnp.sin(angles))], axis=0
    )
    norm_scale = 1.0 / (2 * block_len)
    real_rows = jnp.where(is_first, 1.0, 2.0) * jnp.cos(angles) * norm_scale
    imag_rows = jnp.where(is_first, parity, -2.0 * jnp.sin(angles)) * norm_scale
    inverse = jnp.concatenate([real_rows, imag_rows], axis=0).T
    first_bin = is_first.astype(jnp.float32)
    return (forward, inverse, first_bin)


def spec_product(first_spec, second_spec, first_bin):
    bin_count = first_bin.shape[0]
    first_real, first_imag = (first_spec[..., :bin_count, :], first_spec[..., bin_count:, :])
    second_real, second_imag = (second_spec[..., :bin_count, :], second_spec[..., bin_count:, :])
    others = 1.0 - first_bin
    real_part = first_real * second_real - others * first_imag * second_imag
    imag_part = (
        others * (first_real * second_imag + first_imag * second_real)
        + first_bin * first_imag * second_imag
    )
    return jnp.concatenate([real_part, imag_part], axis=-2)


def conj_product(first_spec, second_spec, first_bin):
    bin_count = first_bin.shape[0]
    first_real, first_imag = (first_spec[..., :bin_count, :], first_spec[..., bin_count:, :])
    second_real, second_imag = (second_spec[..., :bin_count, :], second_spec[..., bin_count:, :])
    others = 1.0 - first_bin
    real_part = first_real * second_real + others * first_imag * second_imag
    imag_part = (
        others * (first_imag * second_real - first_real * second_imag)
        + first_bin * first_imag * second_imag
    )
    return jnp.concatenate([real_part, imag_part], axis=-2)


def transform(dft_table, block_rows):
    return jnp.dot(dft_table, block_rows.astype(jnp.float32), precision=exact_prec)


def body(inputs, gating, filter_taps, skip_gain, w_out, cotangent):
    block_len, channels = inputs.shape
    ctx_count = lax.axis_size("ctx")
    position = lax.axis_index("ctx")
    forward, inverse, first_bin = spectral_tables(block_len)
    first_half = forward[:, :block_len]
    second_half = forward[:, block_len:]
    upstream = lax.dot_general(
        lax.all_gather(cotangent, "ch", axis=1, tiled=True),
        w_out,
        (((1,), (1,)), ((), ())),
        preferred_element_type=jnp.float32,
    )
    gate_wide = gating.astype(jnp.float32)
    grad_mixed = upstream * gate_wide
    signal_all, kernel_all = (
        lax.all_gather(inputs, "ctx", axis=0, tiled=True),
        lax.all_gather(filter_taps, "ctx", axis=0, tiled=True),
    )
    padded = jnp.concatenate(
        [jnp.zeros((block_len, channels), signal_all.dtype), signal_all], axis=0
    )
    own_spec = transform(second_half, grad_mixed)

    def lag_step(lag_index, state_pair):
        running, term_table = state_pair
        segment = lax.dynamic_slice_in_dim(
            padded, (position - lag_index) * block_len, 2 * block_len, 0
        )
        seg_spec = transform(forward, segment)
        kernel_block = lax.dynamic_slice_in_dim(kernel_all, lag_index * block_len, block_len, 0)
        running = running + spec_product(transform(first_half, kernel_block), seg_spec, first_bin)
        term_table = lax.dynamic_update_index_in_dim(
            term_table, conj_product(own_spec, seg_spec, first_bin), lag_index, 0
        )
        return (running, term_table)

    start_terms = jnp.zeros((ctx_count, 2 * block_len, channels), jnp.float32)
    start_spec = jnp.zeros((2 * block_len, channels), jnp.float32)
    running, term_table = lax.fori_loop(0, position + 1, lag_step, (start_spec, start_terms))
    convolved = jnp.dot(inverse[block_len:], running, precision=exact_prec)
    convolved, term_table = (convolved, term_table)
    summed = lax.psum_scatter(
        term_table.astype(jnp.bfloat16), "ctx", scatter_dimension=0, tiled=True
    ).astype(jnp.float32)
    filter_grad = jnp.dot(inverse[:block_len], summed[0], precision=exact_prec)
    mixed_sum = convolved + skip_gain[None, :] * inputs.astype(jnp.float32)
    gated_rows = (gate_wide * mixed_sum).astype(jnp.bfloat16)
    partial_out = jnp.dot(gated_rows, w_out, preferred_element_type=jnp.float32)
    output = lax.psum_scatter(
        partial_out.astype(jnp.bfloat16), "ch", scatter_dimension=1, tiled=True
    )
    return (output, filter_grad)


def solution(mesh):
    return jax.shard_map(
        body,
        mesh=mesh,
        in_specs=(
            P("ctx", "ch"),
            P("ctx", "ch"),
            P("ctx", "ch"),
            P("ch"),
            P("ch", None),
            P("ctx", "ch"),
        ),
        out_specs=(P("ctx", "ch"), P("ctx", "ch")),
        check_vma=False,
    )
```

profile of v0, /device:TPU:2, one launch (start us, length us, event | category | flops | bytes accessed | tf_op | source)
XLA Modules:
  0.0 419.1 jit_solution(11839190690769091835)
XLA Ops:
  7.2 0.7 all-gather.6.cloned.1.call-update
  8.0 0.7 all-gather.8.cloned.1.call-update
  8.7 0.7 all-gather.4.cloned.1.call-update
  9.4 0.0 reduce-scatter.5.cloned.1.call-start
  9.5 1.9 fusion.24
  11.4 2.8 select_multiply_fusion
  14.2 0.9 fusion.12
  15.0 1.1 pad_maximum_fusion
  16.2 36.1 %all-gather.6.cloned.1.call-done = bf16[4096,256]{1,0:T(8,128)(2,1)} async-done(((bf16[256,256]{1,0:T(8,128)(2,1)}), bf16[4096,256]{1,0:T(8,128)(2,1)}) %all-gather.6.cloned.1.call-update) | async-done | bytes 2097168 | tf_op jit(solution)/shard_map/all_gather | solution.py:74
  52.2 3.1 concatenate.17
  55.4 49.4 %all-gather.8.cloned.1.call-done = bf16[256,4096]{1,0:T(8,128)(2,1)} async-done(((bf16[256,256]{1,0:T(8,128)(2,1)}), bf16[256,4096]{1,0:T(8,128)(2,1)}) %all-gather.8.cloned.1.call-update) | async-done | bytes 2097168 | tf_op jit(solution)/shard_map/all_gather | solution.py:66
  104.8 2.3 convolution_multiply_fusion
  107.1 1.5 fusion.14
  108.6 37.2 %all-gather.4.cloned.1.call-done = bf16[4096,256]{1,0:T(8,128)(2,1)} async-done(((bf16[256,256]{1,0:T(8,128)(2,1)}), bf16[4096,256]{1,0:T(8,128)(2,1)}) %all-gather.4.cloned.1.call-update) | async-done | bytes 2097168 | tf_op jit(solution)/shard_map/all_gather | solution.py:75
  145.8 0.8 broadcast_in_dim.64
  146.6 2.3 broadcast_in_dim.65
  149.0 7.6 %while.14 = (s32[]{:T(128)}, f32[512,256]{0,1:T(8,128)}, bf16[16,512,256]{1,2,0:T(8,128)(2,1)}, s32[]{:T(128)}, bf16[4096,256]{1,0:T(8,128)(2,1)}, /*index=5*/f3...) while((s32[]{:T(128)}, f32[512,256]{0,1:T(8,128)}, ...), condition=%wide.region_1.2_spmd.clone.clone, body=%wide.region_0.1_spmd.clone.clone.sunk | while | flops 1210319616 | bytes 8002867 | solution.py:97
  149.0 1.6 convolution_bitcast_fusion.4
  150.6 2.1 convolution_bitcast_fusion.5
  152.7 0.1 multiply_subtract_fusion.2
  152.8 1.9 maximum_add_fusion.2
  154.7 1.1 multiply_add_fusion.4
  155.8 0.7 fusion.48
  156.6 0.0 reduce-scatter.3.cloned.1.call-start
  156.7 2.0 multiply_multiply_fusion
  158.6 0.1 maximum_bitcast_fusion.1
  158.7 1.0 copy-done.2
  159.7 1.0 fusion.8
  160.7 2.1 convolution_convert_fusion
  162.8 167.4 %reduce-scatter.5.cloned.1.call-done = bf16[1,512,256]{1,2,0:T(8,128)(2,1)} async-done(((bf16[16,512,256]{1,2,0:T(8,128)(2,1)}), bf16[1,512,256]{1,2,0:T(8,128)(2,1)}) %reduce-scatter.5.cloned.1.call-update) | async-done | bytes 262160 | tf_op jit(solution)/shard_map/reduce_scatter | solution.py:100
  330.2 2.2 fusion.16
  332.5 80.1 %reduce-scatter.3.cloned.1.call-done = bf16[256,256]{1,0:T(8,128)(2,1)} async-done(((bf16[256,4096]{1,0:T(8,128)(2,1)}), bf16[256,256]{1,0:T(8,128)(2,1)}) %reduce-scatter.3.cloned.1.call-update) | async-done | bytes 131088 | tf_op jit(solution)/shard_map/reduce_scatter | solution.py:107
  (25 shorter events, 0.2 us)
Async XLA Ops:
  7.2 97.6 %copy-start = (bf16[256,4096]{1,0:T(8,128)(2,1)S(1)}, bf16[256,4096]{1,0:T(8,128)(2,1)}, u32[]{:S(2)}) copy-start(bf16[256,4096]{1,0:T(8,128)(2,1)} %param.12) | copy-start | bytes 6291460
  7.2 45.1 %all-gather.6.cloned.1.call-start = ((), (), s32[]{:S(2)}) async-start(), calls=%async_computation.3 | async-start | bytes 2228224 | tf_op jit(solution)/shard_map/all_gather | solution.py:74
  7.9 96.8 %all-gather.8.cloned.1.call-start = ((), (), s32[]{:S(2)}) async-start(), calls=%async_computation.4 | async-start | bytes 2228224 | tf_op jit(solution)/shard_map/all_gather | solution.py:66
  8.7 137.1 %all-gather.4.cloned.1.call-start = ((), (), s32[]{:S(2)}) async-start(), calls=%async_computation.2 | async-start | bytes 2228224 | tf_op jit(solution)/shard_map/all_gather | solution.py:75
  9.4 320.8 %reduce-scatter.5.cloned.1.call-start = ((), (), s32[]{:S(2)}) async-start(), calls=%async_computation.6 | async-start | bytes 4456448 | tf_op jit(solution)/shard_map/reduce_scatter | solution.py:100
  16.2 88.6 %copy-start.5 = (bf16[256,256]{1,0:T(8,128)(2,1)S(1)}, bf16[256,256]{1,0:T(8,128)(2,1)}, u32[]{:S(2)}) copy-start(bf16[256,256]{1,0:T(8,128)(2,1)} %param.9) | copy-start | bytes 393220
  156.5 2.1 copy-start.4
  156.6 3.1 copy-start.1
  156.6 3.1 copy-start.6
  156.6 3.1 copy-start.7
  156.6 256.0 %reduce-scatter.3.cloned.1.call-start = ((), (), s32[]{:S(2)}) async-start(), calls=%async_computation.5 | async-start | bytes 2228224 | tf_op jit(solution)/shard_map/reduce_scatter | solution.py:107
  158.7 1.0 copy-start.2
  162.8 167.5 %copy-start.3 = (f32[512,512]{0,1:T(8,128)S(1)}, f32[512,512]{0,1:T(8,128)}, u32[]{:S(2)}) copy-start(f32[512,512]{0,1:T(8,128)} %copy-done.2) | copy-start | bytes 3145732
Sparse Core Ops, SparseCore 0:
  9.8 42.3 all-gather.5
  54.6 50.0 all-gather.7
  106.6 39.1 all-gather.3
  156.7 173.5 reduce-scatter.4
  334.2 78.3 reduce-scatter.2
where the time goes:
time: 421 us; the launch traced here: 419 us
  waiting for transfers between devices  372 us (88%)
  between operations  13.9 us (3%)
  matrix products  12.8 us (3%)
  other arithmetic  12.6 us (3%)
  local copies, waits for them, and re-layouts  7.34 us (2%)
    reduce_scatter x1, waiting for transfers between devices, body(): lax.psum_scatter(term_table.astype(jnp.bfloat16), 'ctx', scatter_dimensio...  167 us
    reduce_scatter x1, waiting for transfers between devices, body(): lax.psum_scatter(partial_out.astype(jnp.bfloat16), 'ch', scatter_dimensio...  80.1 us
    all_gather x1, waiting for transfers between devices, body(): lax.all_gather(cotangent, 'ch', axis=1, tiled=True)  49.4 us
    all_gather x1, waiting for transfers between devices, body(): lax.all_gather(filter_taps, 'ctx', axis=0, tiled=True)  37.2 us
    all_gather x1, waiting for transfers between devices, body(): lax.all_gather(inputs, 'ctx', axis=0, tiled=True)  36.1 us
  transfers between devices with their start and end apart: 5, of which 5 were waited for; matrix products, arithmetic and copies ran while one was open for 5% of the time, Pallas kernels for 0%

commit v1 on v0

--- a/solution.py
+++ b/solution.py
@@ -5,6 +5,19 @@
 from jax.sharding import PartitionSpec as P
 
 exact_prec = lax.Precision.HIGHEST
+
+
+def ring_gather(x, axis, dim):
+    ways = lax.axis_size(axis)
+    up = [(d, (d + 1) % ways) for d in range(ways)]
+    down = [(d, (d - 1) % ways) for d in range(ways)]
+    earlier, later = ([x], [x])
+    for _ in range(ways // 2):
+        earlier.append(lax.ppermute(earlier[-1], axis, up))
+    for _ in range((ways - 1) // 2):
+        later.append(lax.ppermute(later[-1], axis, down))
+    line = jnp.concatenate([*earlier[::-1], *later[1:]], axis=dim)
+    return jnp.roll(line, (lax.axis_index(axis) - ways // 2) * x.shape[dim], axis=dim)
 
 
 def spectral_tables(block_len):
@@ -72,7 +85,7 @@
     grad_mixed = upstream * gate_wide
     signal_all, kernel_all = (
         lax.all_gather(inputs, "ctx", axis=0, tiled=True),
-        lax.all_gather(filter_taps, "ctx", axis=0, tiled=True),
+        ring_gather(filter_taps, "ctx", 0),
     )
     padded = jnp.concatenate(
         [jnp.zeros((block_len, channels), signal_all.dtype), signal_all], axis=0

time: 421 us -> 385 us (0.914)
  waiting for transfers between devices: 372 us -> 300 us
  starting transfers between devices: 0.19 us -> 21.6 us
  local copies, waits for them, and re-layouts: 7.34 us -> 22 us
    all_gather x1, waiting for transfers between devices: 49.4 us -> 0.01 us  [body(): lax.all_gather(cotangent, 'ch', axis=1, tiled=True)]
    all_gather x1 -> x0, waiting for transfers between devices: 37.2 us -> none  [body(): lax.all_gather(filter_taps, 'ctx', axis=0, tiled=True)]
    ppermute x0 -> x15, waiting for transfers between devices: none -> 21.8 us  [the longest x8 20.5 us: ring_gather(): earlier.append(lax.ppermute(earlier[-1], axis, up))]
    ppermute x0 -> x15, starting transfers between devices: none -> 21.3 us  [the longest x7 21.2 us: ring_gather(): later.append(lax.ppermute(later[-1], axis, down))]
    unnamed x16 -> x83, local copies, waits for them, and re-layouts: 1.01 us -> 14.1 us
    all_gather x1, waiting for transfers between devices: 36.1 us -> 29.6 us  [body(): lax.all_gather(inputs, 'ctx', axis=0, tiled=True)]
  transfers between devices with their start and end apart: 5 -> 19, of which waited for: 5 -> 13; matrix products, arithmetic and copies ran while one was open for 5% -> 8% of each run, Pallas kernels for 0% -> 0%
where the time goes in v1:
time: 385 us; the launch traced here: 383 us
  waiting for transfers between devices  300 us (78%)
  local copies, waits for them, and re-layouts  22 us (6%)
  starting transfers between devices  21.6 us (6%)
  between operations  14.3 us (4%)
  matrix products  12.8 us (3%)
  other arithmetic  12.5 us (3%)
    reduce_scatter x1, waiting for transfers between devices, body(): lax.psum_scatter(term_table.astype(jnp.bfloat16), 'ctx', scatter_dimensio...  168 us
    reduce_scatter x1, waiting for transfers between devices, body(): lax.psum_scatter(partial_out.astype(jnp.bfloat16), 'ch', scatter_dimensio...  80.2 us
    all_gather x1, waiting for transfers between devices, body(): lax.all_gather(inputs, 'ctx', axis=0, tiled=True)  29.6 us
    ppermute x7, starting transfers between devices, ring_gather(): later.append(lax.ppermute(later[-1], axis, down))  21.2 us
    ppermute x8, waiting for transfers between devices, ring_gather(): earlier.append(lax.ppermute(earlier[-1], axis, up))  20.5 us
    unnamed x83, local copies, waits for them, and re-layouts  14.1 us
  transfers between devices with their start and end apart: 19, of which 13 were waited for; matrix products, arithmetic and copies ran while one was open for 8% of the time, Pallas kernels for 0%

profile of v1, /device:TPU:2, one launch (start us, length us, event | category | flops | bytes accessed | tf_op | source)
XLA Modules:
  0.0 383.1 jit_solution(9141744302719295832)
XLA Ops:
  8.0 8.1 %collective-permute-done = bf16[256,256]{1,0:T(8,128)(2,1)S(1)} collective-permute-done((bf16[256,256]{1,0:T(8,128)(2,1)}, bf16[256,256]{1,0:T(8,128)(2,1)S(1)}, u32[]{:S(2)}, u32[]{:S(2)}) %collective-permute-start) | collective-permute-done | bytes 131104 | tf_op jit(solution)/shard_map/ppermute | solution.py:16
  16.1 3.0 collective-permute-start.8
  19.1 2.6 collective-permute-done.1
  21.9 3.0 collective-permute-start.9
  24.9 2.4 collective-permute-done.2
  27.4 3.1 collective-permute-start.10
  30.5 2.4 collective-permute-done.3
  33.1 3.1 collective-permute-start.11
  36.1 2.4 collective-permute-done.4
  38.7 3.1 collective-permute-start.12
  41.7 2.4 collective-permute-done.5
  44.2 2.8 select_multiply_fusion
  47.0 1.9 fusion.24
  49.0 2.9 collective-permute-start.13
  51.9 1.0 pad_maximum_fusion
  54.7 3.1 collective-permute-start.14
  71.2 1.5 constant_dynamic-slice_fusion
  72.7 2.3 convolution_multiply_fusion
  75.1 1.5 fusion.14
  76.5 29.6 %all-gather.3.cloned.1.call-done = bf16[4096,256]{1,0:T(8,128)(2,1)} async-done(((bf16[256,256]{1,0:T(8,128)(2,1)}), bf16[4096,256]{1,0:T(8,128)(2,1)}) %all-gather.3.cloned.1.call-update) | async-done | bytes 2097168 | tf_op jit(solution)/shard_map/all_gather | solution.py:87
  106.1 3.1 concatenate.24
  110.1 2.4 broadcast_in_dim.65
  112.5 7.6 %while.14 = (s32[]{:T(128)}, f32[512,256]{0,1:T(8,128)}, bf16[16,512,256]{1,2,0:T(8,128)(2,1)}, s32[]{:T(128)}, bf16[4096,256]{1,0:T(8,128)(2,1)}, /*index=5*/f3...) while((s32[]{:T(128)}, f32[512,256]{0,1:T(8,128)}, ...), condition=%wide.region_1.2_spmd.clone.clone, body=%wide.region_0.1_spmd.clone.clone.sunk | while | flops 1210319616 | bytes 8002867 | solution.py:110
  112.5 1.6 convolution_bitcast_fusion.4
  114.1 2.1 convolution_bitcast_fusion.5
  116.3 1.9 maximum_add_fusion.2
  118.2 1.1 multiply_add_fusion.4
  120.3 2.0 multiply_multiply_fusion
  124.4 2.1 convolution_convert_fusion
  126.5 167.7 %reduce-scatter.5.cloned.1.call-done = bf16[1,512,256]{1,2,0:T(8,128)(2,1)} async-done(((bf16[16,512,256]{1,2,0:T(8,128)(2,1)}), bf16[1,512,256]{1,2,0:T(8,128)(2,1)}) %reduce-scatter.5.cloned.1.call-update) | async-done | bytes 262160 | tf_op jit(solution)/shard_map/reduce_scatter | solution.py:113
  294.2 2.2 fusion.16
  296.4 80.2 %reduce-scatter.3.cloned.1.call-done = bf16[256,256]{1,0:T(8,128)(2,1)} async-done(((bf16[256,4096]{1,0:T(8,128)(2,1)}), bf16[256,256]{1,0:T(8,128)(2,1)}) %reduce-scatter.3.cloned.1.call-update) | async-done | bytes 131088 | tf_op jit(solution)/shard_map/reduce_scatter | solution.py:120
  (121 shorter events, 20.1 us)
Async XLA Ops:
  7.2 65.6 %copy-start = (bf16[256,4096]{1,0:T(8,128)(2,1)S(1)}, bf16[256,4096]{1,0:T(8,128)(2,1)}, u32[]{:S(2)}) copy-start(bf16[256,4096]{1,0:T(8,128)(2,1)} %param.12) | copy-start | bytes 6291460
  7.2 57.1 %copy-start.7 = (bf16[256,256]{1,0:T(8,128)(2,1)S(1)}, bf16[256,256]{1,0:T(8,128)(2,1)}, u32[]{:S(2)}) copy-start(bf16[256,256]{1,0:T(8,128)(2,1)} %param.10) | copy-start | bytes 393220
  7.2 65.5 %all-gather.5.cloned.1.call-start = ((), (), s32[]{:S(2)}) async-start(), calls=%async_computation.3 | async-start | bytes 2228224 | tf_op jit(solution)/shard_map/all_gather | solution.py:79
  7.9 98.2 %all-gather.3.cloned.1.call-start = ((), (), s32[]{:S(2)}) async-start(), calls=%async_computation.2 | async-start | bytes 2228224 | tf_op jit(solution)/shard_map/all_gather | solution.py:87
  8.0 8.2 %collective-permute-start = (bf16[256,256]{1,0:T(8,128)(2,1)}, bf16[256,256]{1,0:T(8,128)(2,1)S(1)}, u32[]{:S(2)}, u32[]{:S(2)}) collective-permute-start(bf16[256,256]{1,0:T(8,128)(2,1)} %param.10), channel_id=1, source_target_pairs={{0,16},{16,32},{32,48},{48,64},{64,80},{80,96},{96,112},{112,128},... | collective-permute-start | bytes 393224 | tf_op jit(solution)/shard_map/ppermute | solution.py:16
  16.1 5.6 %collective-permute-start.1 = (bf16[256,256]{1,0:T(8,128)(2,1)S(1)}, bf16[256,256]{1,0:T(8,128)(2,1)S(1)}, u32[]{:S(2)}, u32[]{:S(2)}) collective-permute-start(bf16[256,256]{1,0:T(8,128)(2,1)S(1)} %collective-permute-done), channel_id=1, source_target_pairs={{0,16},{16,32},{32,48},{48,64},{64,80},{80,96},{96,112},{112,128},... | collective-permute-start | bytes 393224 | tf_op jit(solution)/shard_map/ppermute | solution.py:16
  16.1 5.8 %collective-permute-start.8 = (bf16[256,256]{1,0:T(8,128)(2,1)}, bf16[256,256]{1,0:T(8,128)(2,1)S(1)}, u32[]{:S(2)}, u32[]{:S(2)}) collective-permute-start(bf16[256,256]{1,0:T(8,128)(2,1)} %param.10), channel_id=1, source_target_pairs={{0,240},{16,0},{32,16},{48,32},{64,48},{80,64},{96,80},{112,96},{1... | collective-permute-start | bytes 393224 | tf_op jit(solution)/shard_map/ppermute | solution.py:18
  21.7 5.6 %collective-permute-start.2 = (bf16[256,256]{1,0:T(8,128)(2,1)S(1)}, bf16[256,256]{1,0:T(8,128)(2,1)S(1)}, u32[]{:S(2)}, u32[]{:S(2)}) collective-permute-start(bf16[256,256]{1,0:T(8,128)(2,1)S(1)} %collective-permute-done.1), channel_id=1, source_target_pairs={{0,16},{16,32},{32,48},{48,64},{64,80},{80,96},{96,112},{112,128},... | collective-permute-start | bytes 393224 | tf_op jit(solution)/shard_map/ppermute | solution.py:16
  21.9 42.5 %copy-start.8 = (bf16[256,256]{1,0:T(8,128)(2,1)}, bf16[256,256]{1,0:T(8,128)(2,1)S(1)}, u32[]{:S(2)}) copy-start(bf16[256,256]{1,0:T(8,128)(2,1)S(1)} %collective-permute-done.8) | copy-start | bytes 393220
  21.9 5.5 %collective-permute-start.9 = (bf16[256,256]{1,0:T(8,128)(2,1)S(1)}, bf16[256,256]{1,0:T(8,128)(2,1)S(1)}, u32[]{:S(2)}, u32[]{:S(2)}) collective-permute-start(bf16[256,256]{1,0:T(8,128)(2,1)S(1)} %collective-permute-done.8), channel_id=1, source_target_pairs={{0,240},{16,0},{32,16},{48,32},{64,48},{80,64},{96,80},{112,96},{1... | collective-permute-start | bytes 393224 | tf_op jit(solution)/shard_map/ppermute | solution.py:18
  27.4 16.8 %copy-start.13 = (bf16[256,256]{1,0:T(8,128)(2,1)}, bf16[256,256]{1,0:T(8,128)(2,1)S(1)}, u32[]{:S(2)}) copy-start(bf16[256,256]{1,0:T(8,128)(2,1)S(1)} %collective-permute-done.2) | copy-start | bytes 393220
  27.4 5.6 %collective-permute-start.3 = (bf16[256,256]{1,0:T(8,128)(2,1)S(1)}, bf16[256,256]{1,0:T(8,128)(2,1)S(1)}, u32[]{:S(2)}, u32[]{:S(2)}) collective-permute-start(bf16[256,256]{1,0:T(8,128)(2,1)S(1)} %collective-permute-done.2), channel_id=1, source_target_pairs={{0,16},{16,32},{32,48},{48,64},{64,80},{80,96},{96,112},{112,128},... | collective-permute-start | bytes 393224 | tf_op jit(solution)/shard_map/ppermute | solution.py:16
  27.4 16.8 %copy-start.11 = (bf16[256,256]{1,0:T(8,128)(2,1)}, bf16[256,256]{1,0:T(8,128)(2,1)S(1)}, u32[]{:S(2)}) copy-start(bf16[256,256]{1,0:T(8,128)(2,1)S(1)} %collective-permute-done.9) | copy-start | bytes 393220
  27.4 5.6 %collective-permute-start.10 = (bf16[256,256]{1,0:T(8,128)(2,1)S(1)}, bf16[256,256]{1,0:T(8,128)(2,1)S(1)}, u32[]{:S(2)}, u32[]{:S(2)}) collective-permute-start(bf16[256,256]{1,0:T(8,128)(2,1)S(1)} %collective-permute-done.9), channel_id=1, source_target_pairs={{0,240},{16,0},{32,16},{48,32},{64,48},{80,64},{96,80},{112,96},{1... | collective-permute-start | bytes 393224 | tf_op jit(solution)/shard_map/ppermute | solution.py:18
  33.0 5.6 %collective-permute-start.4 = (bf16[256,256]{1,0:T(8,128)(2,1)S(1)}, bf16[256,256]{1,0:T(8,128)(2,1)S(1)}, u32[]{:S(2)}, u32[]{:S(2)}) collective-permute-start(bf16[256,256]{1,0:T(8,128)(2,1)S(1)} %collective-permute-done.3), channel_id=1, source_target_pairs={{0,16},{16,32},{32,48},{48,64},{64,80},{80,96},{96,112},{112,128},... | collective-permute-start | bytes 393224 | tf_op jit(solution)/shard_map/ppermute | solution.py:16
  33.0 261.2 %reduce-scatter.5.cloned.1.call-start = ((), (), s32[]{:S(2)}) async-start(), calls=%async_computation.5 | async-start | bytes 4456448 | tf_op jit(solution)/shard_map/reduce_scatter | solution.py:113
  33.1 5.6 %collective-permute-start.11 = (bf16[256,256]{1,0:T(8,128)(2,1)S(1)}, bf16[256,256]{1,0:T(8,128)(2,1)S(1)}, u32[]{:S(2)}, u32[]{:S(2)}) collective-permute-start(bf16[256,256]{1,0:T(8,128)(2,1)S(1)} %collective-permute-done.10), channel_id=1, source_target_pairs={{0,240},{16,0},{32,16},{48,32},{64,48},{80,64},{96,80},{112,96},{1... | collective-permute-start | bytes 393224 | tf_op jit(solution)/shard_map/ppermute | solution.py:18
  38.6 5.6 %collective-permute-start.5 = (bf16[256,256]{1,0:T(8,128)(2,1)S(1)}, bf16[256,256]{1,0:T(8,128)(2,1)S(1)}, u32[]{:S(2)}, u32[]{:S(2)}) collective-permute-start(bf16[256,256]{1,0:T(8,128)(2,1)S(1)} %collective-permute-done.4), channel_id=1, source_target_pairs={{0,16},{16,32},{32,48},{48,64},{64,80},{80,96},{96,112},{112,128},... | collective-permute-start | bytes 393224 | tf_op jit(solution)/shard_map/ppermute | solution.py:16
  38.7 10.3 %collective-permute-start.12 = (bf16[256,256]{1,0:T(8,128)(2,1)S(1)}, bf16[256,256]{1,0:T(8,128)(2,1)}, u32[]{:S(2)}, u32[]{:S(2)}) collective-permute-start(bf16[256,256]{1,0:T(8,128)(2,1)S(1)} %collective-permute-done.11), channel_id=1, source_target_pairs={{0,240},{16,0},{32,16},{48,32},{64,48},{80,64},{96,80},{112,96},{1... | collective-permute-start | bytes 393224 | tf_op jit(solution)/shard_map/ppermute | solution.py:18
  44.2 7.7 %collective-permute-start.6 = (bf16[256,256]{1,0:T(8,128)(2,1)S(1)}, bf16[256,256]{1,0:T(8,128)(2,1)}, u32[]{:S(2)}, u32[]{:S(2)}) collective-permute-start(bf16[256,256]{1,0:T(8,128)(2,1)S(1)} %collective-permute-done.5), channel_id=1, source_target_pairs={{0,16},{16,32},{32,48},{48,64},{64,80},{80,96},{96,112},{112,128},... | collective-permute-start | bytes 393224 | tf_op jit(solution)/shard_map/ppermute | solution.py:16
  49.0 5.8 %collective-permute-start.13 = (bf16[256,256]{1,0:T(8,128)(2,1)}, bf16[256,256]{1,0:T(8,128)(2,1)}, u32[]{:S(2)}, u32[]{:S(2)}) collective-permute-start(bf16[256,256]{1,0:T(8,128)(2,1)} %collective-permute-done.12), channel_id=1, source_target_pairs={{0,240},{16,0},{32,16},{48,32},{64,48},{80,64},{96,80},{112,96},{1... | collective-permute-start | bytes 393224 | tf_op jit(solution)/shard_map/ppermute | solution.py:18
  51.9 5.9 %collective-permute-start.7 = (bf16[256,256]{1,0:T(8,128)(2,1)}, bf16[256,256]{1,0:T(8,128)(2,1)}, u32[]{:S(2)}, u32[]{:S(2)}) collective-permute-start(bf16[256,256]{1,0:T(8,128)(2,1)} %collective-permute-done.6), channel_id=1, source_target_pairs={{0,16},{16,32},{32,48},{48,64},{64,80},{80,96},{96,112},{112,128},... | collective-permute-start | bytes 393224 | tf_op jit(solution)/shard_map/ppermute | solution.py:16
  52.9 11.4 %copy-start.16 = (bf16[256,256]{1,0:T(8,128)(2,1)S(1)}, bf16[256,256]{1,0:T(8,128)(2,1)}, u32[]{:S(2)}) copy-start(bf16[256,256]{1,0:T(8,128)(2,1)} %copy-done.15) | copy-start | bytes 393220
  52.9 11.5 %copy-start.20 = (bf16[256,256]{1,0:T(8,128)(2,1)S(1)}, bf16[256,256]{1,0:T(8,128)(2,1)}, u32[]{:S(2)}) copy-start(bf16[256,256]{1,0:T(8,128)(2,1)} %copy-done.19) | copy-start | bytes 393220
  52.9 15.3 %copy-start.24 = (bf16[256,256]{1,0:T(8,128)(2,1)S(1)}, bf16[256,256]{1,0:T(8,128)(2,1)}, u32[]{:S(2)}) copy-start(bf16[256,256]{1,0:T(8,128)(2,1)} %copy-done.23) | copy-start | bytes 393220
  52.9 15.3 %copy-start.22 = (bf16[256,256]{1,0:T(8,128)(2,1)S(1)}, bf16[256,256]{1,0:T(8,128)(2,1)}, u32[]{:S(2)}) copy-start(bf16[256,256]{1,0:T(8,128)(2,1)} %copy-done.21) | copy-start | bytes 393220
  53.0 15.3 %copy-start.18 = (bf16[256,256]{1,0:T(8,128)(2,1)S(1)}, bf16[256,256]{1,0:T(8,128)(2,1)}, u32[]{:S(2)}) copy-start(bf16[256,256]{1,0:T(8,128)(2,1)} %copy-done.17) | copy-start | bytes 393220
  53.0 15.3 %copy-start.14 = (bf16[256,256]{1,0:T(8,128)(2,1)S(1)}, bf16[256,256]{1,0:T(8,128)(2,1)}, u32[]{:S(2)}) copy-start(bf16[256,256]{1,0:T(8,128)(2,1)} %copy-done.13) | copy-start | bytes 393220
  53.0 15.3 %copy-start.10 = (bf16[256,256]{1,0:T(8,128)(2,1)S(1)}, bf16[256,256]{1,0:T(8,128)(2,1)}, u32[]{:S(2)}) copy-start(bf16[256,256]{1,0:T(8,128)(2,1)} %copy-done.9) | copy-start | bytes 393220
  54.7 11.6 %collective-permute-start.14 = (bf16[256,256]{1,0:T(8,128)(2,1)}, bf16[256,256]{1,0:T(8,128)(2,1)S(1)}, u32[]{:S(2)}, u32[]{:S(2)}) collective-permute-start(bf16[256,256]{1,0:T(8,128)(2,1)} %collective-permute-done.13), channel_id=1, source_target_pairs={{0,240},{16,0},{32,16},{48,32},{64,48},{80,64},{96,80},{112,96},{1... | collective-permute-start | bytes 393224 | tf_op jit(solution)/shard_map/ppermute | solution.py:18
  120.1 256.5 %reduce-scatter.3.cloned.1.call-start = ((), (), s32[]{:S(2)}) async-start(), calls=%async_computation.4 | async-start | bytes 2228224 | tf_op jit(solution)/shard_map/reduce_scatter | solution.py:120
  124.4 169.8 %copy-start.3 = (f32[512,512]{0,1:T(8,128)S(1)}, f32[512,512]{0,1:T(8,128)}, u32[]{:S(2)}) copy-start(f32[512,512]{0,1:T(8,128)} %copy-done.2) | copy-start | bytes 3145732
  (13 other events, 77.9 us)
Sparse Core Ops, SparseCore 0:
  10.4 54.6 all-gather.4
  66.9 39.1 all-gather.2
  120.2 173.9 reduce-scatter.4
  298.2 78.3 reduce-scatter.2
